TPU v7x, 256 devices: a whole 4x4x8 slice. The times are simulated.
256 devices in a mesh: dp: 2 (over y_hi), retr: 16 (over x, y_lo, core), tensor: 8 (over z).
Axes of the slice: x: 4, y: 4 (y_hi: 2, y_lo: 2; y = y_hi * 2 + y_lo), z: 8, core: 2. Of those that a mesh axis runs over, the one named last changes fastest.
Arguments:
- hidden_in: bfloat16 [16384, 4096], P(('dp', 'retr'), 'tensor'), may hold values from -12 to 12
- norm_gain: float32 [4096], replicated, may hold values from 0.1 to 1.9
- nbr_table: int32 [256, 2], P(('dp', 'retr')), may hold values from 0 to 63, as said below
- encodings: bfloat16 [64, 128, 1024], P('retr'), may hold values from -21 to 21
- enc_mask: int32 [64, 4], P('retr'), may hold values from 0 to 1, as said below
- w_query: bfloat16 [4096, 4096], P(None, 'tensor'), may hold values from -0.02703125 to 0.02703125
- w_key: bfloat16 [1024, 4096], P(None, 'tensor'), may hold values from -0.1021875 to 0.1021875
- w_value: bfloat16 [1024, 4096], P(None, 'tensor'), may hold values from -0.1875 to 0.1875
- w_out: bfloat16 [4096, 4096], P('tensor'), may hold values from -0.125 to 0.125
Outputs:
- mixed: bfloat16 [16384, 4096], P(('dp', 'retr'), 'tensor')
Inputs may be any that keep to these rules, and one draw needn't show every extreme that they name: `nbr_table`: each aligned block of 8 table rows (the rows of one device) holds 16 distinct ids; at most 2 of them share the value id // 4, and in every block some value of id // 4 has exactly 2. `enc_mask`: in each row the ones come first; the first entry is 1.
All inputs are finite; a program needn't handle non-finite values.
Results may differ from a plain program's by a relative error of at most 0.012.
The roundings to bfloat16 on the way count: a program that leaves them out, or rounds other values in their place, can miss the bound.
Values may be sent and summed in bfloat16 or wider, within the bound.
No kernel may reach another device: no remote copies, remote signals or barrier semaphores. Data moves between devices by JAX's collectives and lax.ppermute only.
A program may use at most 128 MiB of HBM per device.

v0:
```python
import math
import jax
import jax.numpy as jnp
from jax import lax
from jax.sharding import PartitionSpec as P

HD = 128
NBRS = 2
BLOCK = 32


def attend_gathered(queries, key_value, selected_marks, segment_count, head_cols):
    tok_rows = queries.shape[0]
    head_count = head_cols // HD
    entry_keys = key_value.shape[0] // segment_count * key_value.shape[1]
    mask_cols = selected_marks.shape[1]
    key_block = key_value[:, :, :head_cols].reshape(segment_count, entry_keys, head_count, HD)
    value_block = key_value[:, :, head_cols:].reshape(segment_count, entry_keys, head_count, HD)
    key_live = (
        jnp.repeat(selected_marks.reshape(segment_count, NBRS * mask_cols), BLOCK, axis=1) > 0
    )
    query_block = queries.reshape(segment_count, tok_rows // segment_count, head_count, HD)
    factor = 1.0 / math.sqrt(HD)
    scores = (
        jnp.einsum("cqhd,ckhd->chqk", query_block, key_block, preferred_element_type=jnp.float32)
        * factor
    )
    key_open = key_live[:, None, None, :]
    scores = jnp.where(key_open, scores, -1e30)
    row_max = jnp.max(scores, axis=-1, keepdims=True)
    weights = jnp.exp(scores - row_max) * key_open.astype(jnp.float32)
    probabilities = (weights / jnp.sum(weights, axis=-1, keepdims=True)).astype(jnp.bfloat16)
    attended = jnp.einsum(
        "chqk,ckhd->cqhd", probabilities, value_block, preferred_element_type=jnp.float32
    )
    return attended.astype(jnp.bfloat16).reshape(tok_rows, head_cols)


def local(hidden_in, norm_gain, nbr_table, encodings, enc_mask, w_query, w_key, w_value, w_out):
    gathered = lax.all_gather(hidden_in, "tensor", axis=1, tiled=True)
    widened = gathered.astype(jnp.float32)
    mean_sq = jnp.mean(widened * widened, axis=-1, keepdims=True)
    normed = (widened * lax.rsqrt(mean_sq + 1e-05) * norm_gain).astype(jnp.bfloat16)
    queries = jnp.dot(normed, w_query, preferred_element_type=jnp.float32).astype(jnp.bfloat16)
    w_both = jnp.concatenate([w_key, w_value], axis=1)
    segment_count = nbr_table.shape[0]
    entry_len = encodings.shape[1]
    enc_width = encodings.shape[2]
    head_cols = w_key.shape[1]
    wanted = nbr_table.reshape(-1)
    need_count = wanted.shape[0]
    live_marks = enc_mask.astype(jnp.bfloat16)
    entry_rows = lax.all_gather(encodings, "retr", axis=0, tiled=True)
    entry_marks = lax.all_gather(live_marks, "retr", axis=0, tiled=True)
    piece_count = entry_rows.shape[0]
    one_hot = (wanted[:, None] == jnp.arange(piece_count, dtype=jnp.int32)[None, :]).astype(
        jnp.bfloat16
    )
    picked = jnp.einsum(
        "jn,nre->jre", one_hot, entry_rows, preferred_element_type=jnp.float32
    ).astype(jnp.bfloat16)
    picked_marks = jnp.dot(one_hot, entry_marks, preferred_element_type=jnp.float32).astype(
        jnp.bfloat16
    )
    key_value = jnp.dot(
        picked.reshape(need_count * entry_len, enc_width),
        w_both,
        preferred_element_type=jnp.float32,
    )
    key_value = key_value.astype(jnp.bfloat16).reshape(need_count, entry_len, 2 * head_cols)
    attended = attend_gathered(queries, key_value, picked_marks, segment_count, head_cols)
    partial_value = jnp.dot(attended, w_out, preferred_element_type=jnp.float32)
    summed = lax.psum_scatter(partial_value, "tensor", scatter_dimension=1, tiled=True)
    return (hidden_in.astype(jnp.float32) + summed).astype(jnp.bfloat16)


def solution(mesh):
    in_specs = (
        P(("dp", "retr"), "tensor"),
        P(),
        P(("dp", "retr"), None),
        P("retr", None, None),
        P("retr", None),
        P(None, "tensor"),
        P(None, "tensor"),
        P(None, "tensor"),
        P("tensor", None),
    )
    out_specs = P(("dp", "retr"), "tensor")
    return jax.shard_map(local, mesh=mesh, in_specs=in_specs, out_specs=out_specs, check_vma=False)
```

profile of v0, /device:TPU:1, one launch (start us, length us, event | category | flops | bytes accessed | tf_op | source)
XLA Modules:
  0.0 318.5 jit_solution(9526612523659051779)
XLA Ops:
  6.5 0.7 all-gather.6.cloned.1.call-update
  7.3 0.7 all-gather.4.cloned.1.call-update
  8.1 0.8 copy.24
  8.9 0.7 convert_bitcast_fusion
  9.6 21.0 %all-gather = bf16[16,4,4]{2,1,0:T(4,128)(2,1)S(1)} all-gather(bf16[1,4,4]{2,1,0:T(4,128)(2,1)S(1)} %convert_bitcast_fusion), channel_id=1, replica_groups=mesh['dp'=2,'retr'=16,'tensor'=8] {'retr'}, dimensions={0}, use_global_device_ids=true | all-gather | bytes 544 | tf_op jit(solution)/shard_map/all_gather | solution.py:54
  30.6 0.2 fusion.30
  31.2 36.4 %all-gather.6.cloned.1.call-done = bf16[512,4096]{1,0:T(8,128)(2,1)} async-done(((bf16[512,512]{1,0:T(8,128)(2,1)}), bf16[512,4096]{1,0:T(8,128)(2,1)}) %all-gather.6.cloned.1.call-update) | async-done | bytes 4194320 | tf_op jit(solution)/shard_map/all_gather | solution.py:40
  67.5 3.2 %fusion.3 = f32[512]{0:T(512)S(1)} fusion(bf16[512,4096]{1,0:T(8,128)(2,1)} %all-gather.6.cloned.1.call-done), kind=kLoop, calls=%fused_computation.5 | loop fusion | flops 6290944 | bytes 4196352 | tf_op jit(solution)/shard_map/reduce_sum | solution.py:42
  70.8 0.2 copy-done.1
  71.0 4.6 %fusion.24 = bf16[512,512]{1,0:T(8,128)(2,1)S(1)} fusion(bf16[4096,512]{1,0:T(8,128)(2,1)} %param.14, bf16[512,4096]{1,0:T(8,128)(2,1)S(1)} %copy-done.1, f32[4096]{0:T(1024)S(1)} %copy-done.6, f32[512]{0:T(512)S(1)} %add_rsqrt_fusion), kind=kOutput, calls=%fused_computation.25 | convolution fusion | flops 2156134400 | bytes 8931328 | tf_op jit(solution)/shard_map/dot_general | solution.py:44
  75.6 0.1 reshape.49
  75.7 87.0 %all-gather.4.cloned.1.call-done = bf16[64,128,1024]{2,1,0:T(8,128)(2,1)} async-done(((bf16[4,128,1024]{2,1,0:T(8,128)(2,1)}), bf16[64,128,1024]{2,1,0:T(8,128)(2,1)}) %all-gather.4.cloned.1.call-update) | async-done | bytes 16777232 | tf_op jit(solution)/shard_map/all_gather | solution.py:53
  162.7 23.7 %fusion.10 = bf16[16,128,1024]{2,0,1:T(8,128)(2,1)S(1)} fusion(bf16[64,128,1024]{2,1,0:T(8,128)(2,1)} %all-gather.4.cloned.1.call-done, s32[16]{0:T(128)S(1)} %eq.15), kind=kOutput, calls=%fused_computation.12 | convolution fusion | flops 270533632 | bytes 20971584 | tf_op jit(solution)/shard_map/jn,nre->jre/dot_general | solution.py:59
  186.4 2.5 copy.26
  189.0 5.0 %convolution_convert_fusion = bf16[2048,1024]{1,0:T(8,128)(2,1)S(1)} fusion(bf16[2048,1024]{1,0:T(8,128)(2,1)S(1)} %bitcast.20, bf16[1024,512]{1,0:T(8,128)(2,1)S(1)} %copy-done.4, bf16[1024,512]{1,0:T(8,128)(2,1)S(1)} %copy-done.5), kind=kOutput, calls=%fused_computation.11 | convolution fusion | flops 4301258752 | bytes 10485760 | tf_op jit(solution)/shard_map/dot_general | solution.py:65
  194.0 1.8 fusion.46
  195.8 4.0 %reshape.55 = bf16[8,256,4,128]{3,2,1,0:T(4,128)(2,1)} reshape(bf16[16,128,512]{2,1,0:T(8,128)(2,1)} %get-tuple-element.5) | data formatting | bytes 4194304 | tf_op jit(solution)/shard_map/reshape | solution.py:17
  199.8 2.0 reshape.56
  201.8 4.1 %fusion.47 = (f32[8,4,64]{2,1,0:T(4,128)S(1)}, f32[8,4,64,256]{3,2,1,0:T(8,128)}) fusion(f32[8,256]{1,0:T(8,128)S(1)} %convert_element_type.53, pred[8,256]{1,0:T(8,128)(4,1)S(1)} %gt.23, bf16[8,256,4,128]{3,2,1,0:T(4,128)(2,1)} %reshape.55, bf16[8,64,4,128]{3,2,1,0:T(4,128)(2,1)S(1)} %reshape.49), kind=kOutput, calls=%fused_computation.48 | convolution fusion | flops 136839424 | bytes 4737024 | tf_op jit(solution)/shard_map/sub | solution.py:31
  206.0 2.3 fusion.27
  208.3 0.4 copy.33
  208.8 5.6 %fusion.35 = f32[512,4096]{1,0:T(8,128)} fusion(bf16[512,4096]{1,0:T(8,128)(2,1)S(1)} %copy-done, bf16[64,8,4,128]{3,2,1,0:T(4,128)(2,1)S(1)} %bitcast.21), kind=kOutput, calls=%fused_computation.34 | convolution fusion | flops 2147483648 | bytes 13107200 | tf_op jit(solution)/shard_map/dot_general | solution.py:72
  214.4 95.4 %reduce-scatter.2.cloned.1.call-done = f32[512,512]{1,0:T(8,128)} async-done(((f32[512,4096]{1,0:T(8,128)}), f32[512,512]{1,0:T(8,128)}) %reduce-scatter.2.cloned.1.call-update) | async-done | bytes 1048592 | tf_op jit(solution)/shard_map/reduce_scatter | solution.py:73
  309.8 2.2 add_convert_fusion
  (24 shorter events, 0.7 us)
Async XLA Ops:
  6.5 64.2 %copy-start.6 = (f32[4096]{0:T(1024)S(1)}, f32[4096]{0:T(1024)}, u32[]{:S(2)}) copy-start(f32[4096]{0:T(1024)} %param.10) | copy-start | bytes 49156
  6.5 61.0 %all-gather.6.cloned.1.call-start = ((), (), s32[]{:S(2)}) async-start(), calls=%async_computation.2 | async-start | bytes 4718592 | tf_op jit(solution)/shard_map/all_gather | solution.py:40
  7.3 155.4 %all-gather.4.cloned.1.call-start = ((), (), s32[]{:S(2)}) async-start(), calls=%async_computation.1 | async-start | bytes 17825792 | tf_op jit(solution)/shard_map/all_gather | solution.py:53
  8.0 301.8 %reduce-scatter.2.cloned.1.call-start = ((), (), s32[]{:S(2)}) async-start(), calls=%async_computation.3 | async-start | bytes 9437184 | tf_op jit(solution)/shard_map/reduce_scatter | solution.py:73
  67.5 3.4 %copy-start.1 = (bf16[512,4096]{1,0:T(8,128)(2,1)S(1)}, bf16[512,4096]{1,0:T(8,128)(2,1)}, u32[]{:S(2)}) copy-start(bf16[512,4096]{1,0:T(8,128)(2,1)} %all-gather.6.cloned.1.call-done) | copy-start | bytes 12582916
  186.4 2.6 copy-start.4
  186.4 2.6 copy-start.5
  201.8 4.2 %copy-start.2 = (bf16[8,256,4,128]{3,2,1,0:T(4,128)(2,1)S(1)}, bf16[8,256,4,128]{3,2,1,0:T(4,128)(2,1)}, u32[]{:S(2)}) copy-start(bf16[8,256,4,128]{3,2,1,0:T(4,128)(2,1)} %reshape.56) | copy-start | bytes 6291460
  206.0 2.8 copy-start
  214.4 95.4 %copy-start.3 = (bf16[512,512]{1,0:T(8,128)(2,1)S(1)}, bf16[512,512]{1,0:T(8,128)(2,1)}, u32[]{:S(2)}) copy-start(bf16[512,512]{1,0:T(8,128)(2,1)} %param.9) | copy-start | bytes 1572868
Sparse Core Ops, SparseCore 0:
  9.1 58.3 all-gather.5
  69.4 93.2 all-gather.3
  214.5 95.2 reduce-scatter.1
where the time goes:
time: 319 us
  waiting for transfers between devices  220 us (69%)
  matrix products  45.5 us (14%)
  blocking collectives  21 us (7%)
  between operations  13.2 us (4%)
  local copies, waits for them, and re-layouts  12.5 us (4%)
  other arithmetic  6.11 us (2%)
    reduce_scatter x1, waiting for transfers between devices, local(): lax.psum_scatter(partial_value, 'tensor', scatter_dimension=1, tiled=True)  95.4 us
    all_gather x1, waiting for transfers between devices, local(): entry_rows = lax.all_gather(encodings, 'retr', axis=0, tiled=True)  87 us
    all_gather x1, waiting for transfers between devices, local(): gathered = lax.all_gather(hidden_in, 'tensor', axis=1, tiled=True)  36.4 us
    dot_general x1, matrix products, local(): jnp.einsum('jn,nre->jre', one_hot, entry_rows, preferred_element_type=jnp...  23.7 us
    all_gather x1, blocking collectives, local(): entry_marks = lax.all_gather(live_marks, 'retr', axis=0, tiled=True)  21 us
  transfers between devices with their start and end apart: 3, of which 3 were waited for; matrix products, arithmetic and copies ran while one was open for 3% of the time, Pallas kernels for 0%

commit v1 on v0

--- a/solution.py
+++ b/solution.py
@@ -37,7 +37,11 @@
 
 
 def local(hidden_in, norm_gain, nbr_table, encodings, enc_mask, w_query, w_key, w_value, w_out):
-    gathered = lax.all_gather(hidden_in, "tensor", axis=1, tiled=True)
+    produce_trees = lambda unit, dim_i: jnp.concatenate(
+        lax.all_to_all(jnp.stack([unit for _ in range(lax.axis_size("tensor"))]), "tensor", 0, 0),
+        dim_i,
+    )
+    gathered = produce_trees(hidden_in, 1)
     widened = gathered.astype(jnp.float32)
     mean_sq = jnp.mean(widened * widened, axis=-1, keepdims=True)
     normed = (widened * lax.rsqrt(mean_sq + 1e-05) * norm_gain).astype(jnp.bfloat16)

time: 319 us -> 278 us (0.87)
  waiting for transfers between devices: 220 us -> 167 us
  starting transfers between devices: 0.08 us -> 9.18 us
    all_gather x1, waiting for transfers between devices: 87 us -> 0.02 us  [local(): entry_rows = lax.all_gather(encodings, 'retr', axis=0, tiled=True)]
    all_to_all x0 -> x1, waiting for transfers between devices: none -> 75.5 us  [local(): lax.all_to_all(jnp.stack([unit for _ in range(lax.axis_size('tensor'))]),...]
    all_gather x1 -> x0, waiting for transfers between devices: 36.4 us -> none  [local(): gathered = lax.all_gather(hidden_in, 'tensor', axis=1, tiled=True)]
    all_to_all x0 -> x1, starting transfers between devices: none -> 9.13 us  [local(): lax.all_to_all(jnp.stack([unit for _ in range(lax.axis_size('tensor'))]),...]
    reduce_scatter x1, waiting for transfers between devices: 95.4 us -> 91.2 us  [local(): lax.psum_scatter(partial_value, 'tensor', scatter_dimension=1, tiled=True)]
  transfers between devices with their start and end apart: 3 -> 3, of which waited for: 3 -> 2; matrix products, arithmetic and copies ran while one was open for 3% -> 5% of each run, Pallas kernels for 0% -> 0%
where the time goes in v1:
time: 278 us
  waiting for transfers between devices  167 us (60%)
  matrix products  43.6 us (16%)
  blocking collectives  20.5 us (7%)
  local copies, waits for them, and re-layouts  15.3 us (6%)
  between operations  13.5 us (5%)
  starting transfers between devices  9.18 us (3%)
  other arithmetic  8.45 us (3%)
    reduce_scatter x1, waiting for transfers between devices, local(): lax.psum_scatter(partial_value, 'tensor', scatter_dimension=1, tiled=True)  91.2 us
    all_to_all x1, waiting for transfers between devices, local(): lax.all_to_all(jnp.stack([unit for _ in range(lax.axis_size('tensor'))]),...  75.5 us
    dot_general x1, matrix products, local(): jnp.einsum('jn,nre->jre', one_hot, entry_rows, preferred_element_type=jnp...  23.7 us
    all_gather x1, blocking collectives, local(): entry_marks = lax.all_gather(live_marks, 'retr', axis=0, tiled=True)  20.5 us
    all_to_all x1, starting transfers between devices, local(): lax.all_to_all(jnp.stack([unit for _ in range(lax.axis_size('tensor'))]),...  9.13 us
    dot_general x1, matrix products, local(): partial_value = jnp.dot(attended, w_out, preferred_element_type=jnp.float32)  5.6 us
  transfers between devices with their start and end apart: 3, of which 2 were waited for; matrix products, arithmetic and copies ran while one was open for 5% of the time, Pallas kernels for 0%

profile of v1, /device:TPU:1, one launch (start us, length us, event | category | flops | bytes accessed | tf_op | source)
XLA Modules:
  0.0 278.0 jit_solution(12255420430768097233)
XLA Ops:
  6.5 0.7 all-gather.3.cloned.1.call-update
  7.3 1.3 copy.30
  8.5 2.3 stack.2
  10.9 9.1 %all-to-all-start = ((bf16[8,512,512]{1,2,0:T(8,128)(2,1)}), bf16[8,512,512]{1,2,0:T(8,128)(2,1)}, u32[]{:S(2)}, u32[]{:S(2)}) async-start(bf16[8,512,512]{1,2,0:T(8,128)(2,1)} %stack.2), calls=%async_computation | async-start | bytes 8388608 | tf_op jit(solution)/shard_map/all_to_all | solution.py:41
  20.2 20.5 %all-gather = bf16[16,4,4]{2,1,0:T(4,128)(2,1)S(1)} all-gather(bf16[1,4,4]{2,1,0:T(4,128)(2,1)S(1)} %convert_bitcast_fusion), channel_id=1, replica_groups=mesh['dp'=2,'retr'=16,'tensor'=8] {'retr'}, dimensions={0}, use_global_device_ids=true | all-gather | bytes 544 | tf_op jit(solution)/shard_map/all_gather | solution.py:58
  40.8 0.2 fusion.22
  41.3 75.5 %all-to-all-done = bf16[8,512,512]{1,2,0:T(8,128)(2,1)} async-done(((bf16[8,512,512]{1,2,0:T(8,128)(2,1)}), bf16[8,512,512]{1,2,0:T(8,128)(2,1)}, u32[]{:S(2)}, u32[]{:S(2)}) %all-to-all-start) | async-done | bytes 4194336 | tf_op jit(solution)/shard_map/all_to_all | solution.py:41
  116.8 3.1 %multiply_reduce_fusion = f32[512]{0:T(512)S(1)} fusion(bf16[8,512,512]{1,2,0:T(8,128)(2,1)} %all-to-all-done), kind=kLoop, calls=%fused_computation.6 | loop fusion | flops 6290944 | bytes 4196352 | tf_op jit(solution)/shard_map/reduce_sum | solution.py:46
  120.0 3.1 %fusion.4 = bf16[512,4096]{0,1:T(8,128)(2,1)S(1)} fusion(f32[4096]{0:T(1024)S(1)} %copy-done.3, f32[512]{0:T(512)S(1)} %add_rsqrt_fusion, bf16[8,512,512]{1,2,0:T(8,128)(2,1)} %all-to-all-done), kind=kLoop, calls=%fused_computation.5 | loop fusion | flops 8388608 | bytes 8407040 | tf_op jit(solution)/shard_map/convert_element_type | solution.py:47
  123.1 0.3 copy-done.6
  123.5 2.4 convolution_convert_fusion.1
  125.8 0.1 reshape.55
  126.0 23.7 %fusion.5 = bf16[16,128,1024]{2,0,1:T(8,128)(2,1)S(1)} fusion(bf16[64,128,1024]{2,1,0:T(8,128)(2,1)} %all-gather.3.cloned.1.call-done, s32[16]{0:T(128)S(1)} %eq.15), kind=kOutput, calls=%fused_computation.8 | convolution fusion | flops 270533632 | bytes 20971584 | tf_op jit(solution)/shard_map/jn,nre->jre/dot_general | solution.py:63
  149.7 2.3 copy.27
  152.1 5.3 %convolution_convert_fusion = bf16[2048,1024]{1,0:T(8,128)(2,1)S(1)} fusion(bf16[2048,1024]{1,0:T(8,128)(2,1)S(1)} %bitcast.29, bf16[1024,512]{1,0:T(8,128)(2,1)S(1)} %copy-done.7, bf16[1024,512]{1,0:T(8,128)(2,1)S(1)} %copy-done.8), kind=kOutput, calls=%fused_computation.7 | convolution fusion | flops 4301258752 | bytes 10485760 | tf_op jit(solution)/shard_map/dot_general | solution.py:69
  157.4 1.8 fusion.38
  159.2 4.0 %reshape.62 = bf16[8,256,4,128]{3,2,1,0:T(4,128)(2,1)} reshape(bf16[16,128,512]{2,1,0:T(8,128)(2,1)} %get-tuple-element.5) | data formatting | bytes 4194304 | tf_op jit(solution)/shard_map/reshape | solution.py:17
  163.1 2.0 reshape.63
  165.2 4.2 %fusion.39 = (f32[8,4,64]{2,1,0:T(4,128)S(1)}, f32[8,4,64,256]{3,2,1,0:T(8,128)}) fusion(f32[8,256]{1,0:T(8,128)S(1)} %convert_element_type.66, pred[8,256]{1,0:T(8,128)(4,1)S(1)} %gt.23, bf16[8,256,4,128]{3,2,1,0:T(4,128)(2,1)} %reshape.62, bf16[8,64,4,128]{3,2,1,0:T(4,128)(2,1)S(1)} %reshape.55), kind=kOutput, calls=%fused_computation.44 | convolution fusion | flops 136839424 | bytes 4737024 | tf_op jit(solution)/shard_map/sub | solution.py:31
  169.3 2.3 fusion.19
  171.6 0.4 copy.35
  172.2 5.6 %fusion.27 = f32[512,4096]{1,0:T(8,128)} fusion(bf16[512,4096]{1,0:T(8,128)(2,1)S(1)} %copy-done, bf16[64,8,4,128]{3,2,1,0:T(4,128)(2,1)S(1)} %bitcast.30), kind=kOutput, calls=%fused_computation.30 | convolution fusion | flops 2147483648 | bytes 13107200 | tf_op jit(solution)/shard_map/dot_general | solution.py:76
  177.8 91.2 %reduce-scatter.2.cloned.1.call-done = f32[512,512]{1,0:T(8,128)} async-done(((f32[512,4096]{1,0:T(8,128)}), f32[512,512]{1,0:T(8,128)}) %reduce-scatter.2.cloned.1.call-update) | async-done | bytes 1048592 | tf_op jit(solution)/shard_map/reduce_scatter | solution.py:77
  269.0 2.2 add_convert_fusion
  (30 shorter events, 0.8 us)
Async XLA Ops:
  6.5 119.4 %all-gather.3.cloned.1.call-start = ((), (), s32[]{:S(2)}) async-start(), calls=%async_computation.2 | async-start | bytes 17825792 | tf_op jit(solution)/shard_map/all_gather | solution.py:57
  10.9 9.2 %copy-start.5 = (s32[8,2]{0,1:T(2,128)S(1)}, s32[8,2]{0,1:T(2,128)}, u32[]{:S(2)}) copy-start(s32[8,2]{0,1:T(2,128)} %param.11) | copy-start | bytes 196
  10.9 9.4 %copy-start.4 = (s32[4,4]{1,0:T(4,128)S(1)}, s32[4,4]{1,0:T(4,128)}, u32[]{:S(2)}) copy-start(s32[4,4]{1,0:T(4,128)} %param.13) | copy-start | bytes 196
  10.9 106.0 %all-to-all-start = ((bf16[8,512,512]{1,2,0:T(8,128)(2,1)}), bf16[8,512,512]{1,2,0:T(8,128)(2,1)}, u32[]{:S(2)}, u32[]{:S(2)}) async-start(bf16[8,512,512]{1,2,0:T(8,128)(2,1)} %stack.2), calls=%async_computation | async-start | bytes 8388608 | tf_op jit(solution)/shard_map/all_to_all | solution.py:41
  20.0 100.0 %copy-start.3 = (f32[4096]{0:T(1024)S(1)}, f32[4096]{0:T(1024)}, u32[]{:S(2)}) copy-start(f32[4096]{0:T(1024)} %param.10) | copy-start | bytes 49156
  20.0 249.0 %reduce-scatter.2.cloned.1.call-start = ((), (), s32[]{:S(2)}) async-start(), calls=%async_computation.3 | async-start | bytes 9437184 | tf_op jit(solution)/shard_map/reduce_scatter | solution.py:77
  120.0 3.5 %copy-start.6 = (bf16[4096,512]{1,0:T(8,128)(2,1)S(1)}, bf16[4096,512]{1,0:T(8,128)(2,1)}, u32[]{:S(2)}) copy-start(bf16[4096,512]{1,0:T(8,128)(2,1)} %param.14) | copy-start | bytes 12582916
  149.7 2.3 copy-start.7
  149.7 2.4 copy-start.8
  165.2 4.2 %copy-start.1 = (bf16[8,256,4,128]{3,2,1,0:T(4,128)(2,1)S(1)}, bf16[8,256,4,128]{3,2,1,0:T(4,128)(2,1)}, u32[]{:S(2)}) copy-start(bf16[8,256,4,128]{3,2,1,0:T(4,128)(2,1)} %reshape.63) | copy-start | bytes 6291460
  169.3 2.8 %copy-start = (bf16[512,4096]{1,0:T(8,128)(2,1)S(1)}, bf16[512,4096]{1,0:T(8,128)(2,1)}, u32[]{:S(2)}) copy-start(bf16[512,4096]{1,0:T(8,128)(2,1)} %param.17) | copy-start | bytes 12582916
  177.8 91.2 %copy-start.2 = (bf16[512,512]{1,0:T(8,128)(2,1)S(1)}, bf16[512,512]{1,0:T(8,128)(2,1)}, u32[]{:S(2)}) copy-start(bf16[512,512]{1,0:T(8,128)(2,1)} %param.9) | copy-start | bytes 1572868
Sparse Core Ops, SparseCore 0:
  9.2 98.3 all-gather.2
  177.9 91.0 reduce-scatter.1
